TPU v7x, 32 devices: a whole 2x2x4 slice. The times are simulated.
32 devices in a mesh: groups: 2 (over y), ctx: 4 (over x, core), dp: 4 (over z).
Axes of the slice: x: 2, y: 2, z: 4, core: 2. Of those that a mesh axis runs over, the one named last changes fastest.
Arguments:
- hidden_in: bfloat16 [8192, 1536], P(('groups', 'ctx', 'dp')), parts along dimension 0, may hold values from -0.119628906 to 0.119628906
- queries: bfloat16 [8192, 1536], P(('groups', 'ctx', 'dp')), parts along dimension 0, may hold values from -60 to 60
- keys: bfloat16 [8192, 256], P(('groups', 'ctx', 'dp')), parts along dimension 0, may hold values from -60 to 60
- values: bfloat16 [8192, 256], P(('groups', 'ctx', 'dp')), parts along dimension 0, may hold values from -6 to 6
- out_grad: bfloat16 [8192, 1536], P(('groups', 'ctx', 'dp')), parts along dimension 0, may hold values from -48 to 48
- segment_ids: int32 [8192], P('groups'), parts along dimension 0, may hold values from 0 to 15, never falling along the last dimension, each value on 1 to 512 neighbouring positions
Outputs:
- query_grad: bfloat16 [8192, 1536], P(('groups', 'ctx', 'dp')), parts along dimension 0
- kv_weight_grad: float32 [3072, 512], P(('groups', 'dp')), parts along dimension 0
There are 2 independent parts, one for each index of `groups`. A program takes and returns all parts, laid end to end along the dimension named above; each array names one. Nothing has to cross between parts.
Inputs may be any that keep to these rules, and one draw needn't show every extreme that they name: `segment_ids`: the ids never fall along the tokens; each rollout takes 1 to 512 consecutive positions, and one takes exactly 512.
All inputs are finite; a program needn't handle non-finite values.
Results may differ from a plain program's by a relative error of at most 0.0049.
Values may be sent and summed in bfloat16 or wider, within the bound.
No kernel may reach another device: no remote copies, remote signals or barrier semaphores. Data moves between devices by JAX's collectives and lax.ppermute only.
A program may use at most 64 MiB of HBM per device.

v0:
```python
import jax
import jax.numpy as jnp
from jax import lax
from jax.sharding import PartitionSpec as P

QUERY_HEADS = 12
KEY_VALUE_HEADS = 2
HEAD_SIZE = 128


def shifted(block, axis, distance):
    devices = range(lax.axis_size(axis))
    route = [(i - distance, i) for i in devices if i - distance in devices]
    return lax.ppermute(block, axis, route)


def window_grads(block_of_query, key_span_window, value_span_window, block_gradient, visible):
    rows_per_block = block_of_query.shape[0]
    rows_in_span = key_span_window.shape[0]
    group_width = QUERY_HEADS // KEY_VALUE_HEADS
    scale = HEAD_SIZE ** (-0.5)
    heads_of_query = block_of_query.reshape(rows_per_block, KEY_VALUE_HEADS, group_width, HEAD_SIZE)
    head_gradients = block_gradient.reshape(rows_per_block, KEY_VALUE_HEADS, group_width, HEAD_SIZE)
    heads_of_key = key_span_window.reshape(rows_in_span, KEY_VALUE_HEADS, HEAD_SIZE)
    heads_of_value = value_span_window.reshape(rows_in_span, KEY_VALUE_HEADS, HEAD_SIZE)
    query_parts = []
    key_pieces = []
    value_pieces = []
    for head_position in range(KEY_VALUE_HEADS):
        query_now = heads_of_query[:, head_position]
        grad_now = head_gradients[:, head_position]
        key_now = heads_of_key[:, head_position]
        value_now = heads_of_value[:, head_position]
        scores = (
            jnp.einsum("tgd,sd->gts", query_now, key_now, preferred_element_type=jnp.float32)
            * scale
        )
        scores = jnp.where(visible[None], scores, -jnp.inf)
        top = jnp.max(scores, axis=-1, keepdims=True)
        expo = jnp.exp(scores - top)
        probs = expo / jnp.sum(expo, axis=-1, keepdims=True)
        probs_low = probs.astype(jnp.bfloat16)
        dprobs = jnp.einsum("tgd,sd->gts", grad_now, value_now, preferred_element_type=jnp.float32)
        delta = jnp.sum(probs * dprobs, axis=-1, keepdims=True)
        dscores_low = (probs * (dprobs - delta)).astype(jnp.bfloat16)
        value_pieces.append(
            jnp.einsum("gts,tgd->sd", probs_low, grad_now, preferred_element_type=jnp.float32)
        )
        key_pieces.append(
            jnp.einsum("gts,tgd->sd", dscores_low, query_now, preferred_element_type=jnp.float32)
            * scale
        )
        query_parts.append(
            jnp.einsum("gts,sd->tgd", dscores_low, key_now, preferred_element_type=jnp.float32)
            * scale
        )
    query_grad = jnp.stack(query_parts, 1).reshape(rows_per_block, QUERY_HEADS * HEAD_SIZE)
    key_gradient = jnp.stack(key_pieces, 1).reshape(rows_in_span, KEY_VALUE_HEADS * HEAD_SIZE)
    value_gradient = jnp.stack(value_pieces, 1).reshape(rows_in_span, KEY_VALUE_HEADS * HEAD_SIZE)
    return (query_grad, jnp.concatenate([key_gradient, value_gradient], 1))


def weight_term(hidden_block, kv_grad):
    return jnp.einsum(
        "td,tc->dc", hidden_block.astype(jnp.float32), kv_grad, precision=lax.Precision.HIGHEST
    )


def on_device(hidden_in, queries, keys, values, out_grad, segment_ids):
    rows_per_block = queries.shape[0]
    cycle_place = lax.axis_index(("ctx", "dp"))
    prev_keys, prev_values = shifted((keys, values), ("ctx", "dp"), 1)
    key_span_window = jnp.concatenate([prev_keys, keys], 0)
    value_span_window = jnp.concatenate([prev_values, values], 0)
    own_segments = lax.dynamic_slice_in_dim(
        segment_ids, cycle_place * rows_per_block, rows_per_block, 0
    )
    prev_segments = lax.dynamic_slice_in_dim(
        segment_ids, jnp.maximum(cycle_place - 1, 0) * rows_per_block, rows_per_block, 0
    )
    key_segments = jnp.concatenate([prev_segments, own_segments], 0)
    query_rows = jnp.arange(rows_per_block, dtype=jnp.int32)[:, None]
    key_cols = jnp.arange(2 * rows_per_block, dtype=jnp.int32)[None, :]
    visible = (key_cols <= query_rows + rows_per_block) & (
        (key_cols >= rows_per_block) | (cycle_place > 0)
    )
    visible = visible & (key_segments[None, :] == own_segments[:, None])
    query_grad, kv_window = window_grads(
        queries, key_span_window, value_span_window, out_grad, visible
    )
    returned = shifted(kv_window[:rows_per_block].astype(jnp.bfloat16), ("ctx", "dp"), -1).astype(
        jnp.float32
    )
    term = weight_term(hidden_in, kv_window[rows_per_block:] + returned)
    total_rows = term.shape[0]
    replica_count = lax.axis_size("dp")
    whole = lax.psum(term, ("ctx", "dp"))
    share = total_rows // replica_count
    weight_grad = lax.dynamic_slice_in_dim(whole, lax.axis_index("dp") * share, share, 0)
    return (query_grad.astype(jnp.bfloat16), weight_grad)


def solution(mesh):
    return jax.shard_map(
        on_device,
        mesh=mesh,
        in_specs=(
            P(("groups", "ctx", "dp"), None),
            P(("groups", "ctx", "dp"), None),
            P(("groups", "ctx", "dp"), None),
            P(("groups", "ctx", "dp"), None),
            P(("groups", "ctx", "dp"), None),
            P("groups"),
        ),
        out_specs=(P(("groups", "ctx", "dp"), None), P(("groups", "dp"), None)),
        check_vma=False,
    )
```

profile of v0, /device:TPU:0, one launch (start us, length us, event | category | flops | bytes accessed | tf_op | source)
XLA Modules:
  0.0 159.0 jit_solution(12490290141752014390)
XLA Ops:
  7.2 1.1 copy.27
  8.3 4.9 %collective-permute-start.1 = (bf16[256,256]{0,1:T(8,128)(2,1)S(1)}, bf16[256,256]{0,1:T(8,128)(2,1)S(1)}, u32[]{:S(2)}, u32[]{:S(2)}) collective-permute-start(bf16[256,256]{0,1:T(8,128)(2,1)S(1)} %copy.27), channel_id=1, source_target_pairs={{0,1},{1,2},{2,3},{3,4},{4,5},{5,6},{6,7},{7,8},{8,9},{9,10},{10,1... | collective-permute-start | bytes 393224 | tf_op jit(solution)/shard_map/ppermute | solution.py:14
  13.2 1.0 copy.22
  14.3 3.5 %collective-permute-start = (bf16[256,256]{0,1:T(8,128)(2,1)S(1)}, bf16[256,256]{0,1:T(8,128)(2,1)S(1)}, u32[]{:S(2)}, u32[]{:S(2)}) collective-permute-start(bf16[256,256]{0,1:T(8,128)(2,1)S(1)} %copy.22), channel_id=1, source_target_pairs={{0,1},{1,2},{2,3},{3,4},{4,5},{5,6},{6,7},{7,8},{8,9},{9,10},{10,1... | collective-permute-start | bytes 393224 | tf_op jit(solution)/shard_map/ppermute | solution.py:14
  17.8 1.4 copy.25
  19.2 1.4 copy.30
  20.6 0.8 fusion.51
  22.9 1.4 fusion.52
  24.3 0.6 fusion.27
  25.0 1.5 fusion.53
  26.5 0.6 fusion.2
  27.1 0.6 fusion.24
  27.8 0.6 fusion.5
  28.9 0.6 fusion.31
  30.0 1.1 copy-done.1
  31.1 0.6 fusion.33
  31.9 1.3 collective-permute-start.2
  33.2 9.2 %collective-permute-done.2 = bf16[256,512]{0,1:T(8,128)(2,1)S(1)} collective-permute-done((bf16[256,512]{0,1:T(8,128)(2,1)S(1)}, bf16[256,512]{0,1:T(8,128)(2,1)S(1)}, u32[]{:S(2)}, u32[]{:S(2)}) %collective-permute-start.2) | collective-permute-done | bytes 262176 | tf_op jit(solution)/shard_map/ppermute | solution.py:14
  42.4 3.1 %convolution_bitcast_fusion = f32[1536,512]{0,1:T(8,128)} fusion(bf16[256,1536]{1,0:T(8,128)(2,1)S(1)} %copy-done, f32[512,256]{0,1:T(8,128)S(1)} %bitcast.147, f32[512,256]{0,1:T(8,128)S(1)} %bitcast.145, bf16[256,512]{0,1:T(8,128)(2,1)S(1)} %collective-permute-done.2), kind=kOutput, calls=%fused_computation.2 | convolution fusion | flops 2416312320 | bytes 5242880 | tf_op jit(solution)/shard_map/td,tc->dc/dot_general | solution.py:64
  45.9 1.8 %fusion.23 = bf16[256,1,6,128]{0,3,2,1:T(8,128)(2,1)S(1)} fusion(bf16[6,256,512]{1,2,0:T(8,128)(2,1)} %copy-done.1, bf16[512,2,128]{0,2,1:T(8,128)(2,1)S(1)} %bitcast.156), kind=kOutput, calls=%fused_computation.36 | convolution fusion | flops 201719808 | bytes 2097152 | tf_op jit(solution)/shard_map/gts,sd->tgd/dot_general | solution.py:54
  47.8 1.2 copy.48
  48.9 100.9 %all-reduce.2.cloned.1.call-done = f32[1536,512]{0,1:T(8,128)} async-done(((f32[1536,512]{0,1:T(8,128)}), f32[1536,512]{0,1:T(8,128)}) %all-reduce.2.cloned.1.call-update) | async-done | bytes 3145744 | tf_op jit(solution)/shard_map/psum | solution.py:97
  149.9 1.2 constant_dynamic-slice_fusion
  151.0 1.1 copy.49
  (22 shorter events, 3.0 us)
Async XLA Ops:
  7.2 35.2 %copy-start = (bf16[256,1536]{1,0:T(8,128)(2,1)S(1)}, bf16[256,1536]{1,0:T(8,128)(2,1)}, u32[]{:S(2)}) copy-start(bf16[256,1536]{1,0:T(8,128)(2,1)} %param.6) | copy-start | bytes 2359300
  7.2 142.7 %all-reduce.2.cloned.1.call-start = ((), (), s32[]{:S(2)}) async-start(), calls=%async_computation | async-start | bytes 6291456 | tf_op jit(solution)/shard_map/psum | solution.py:97
  8.3 18.2 %collective-permute-start.1 = (bf16[256,256]{0,1:T(8,128)(2,1)S(1)}, bf16[256,256]{0,1:T(8,128)(2,1)S(1)}, u32[]{:S(2)}, u32[]{:S(2)}) collective-permute-start(bf16[256,256]{0,1:T(8,128)(2,1)S(1)} %copy.27), channel_id=1, source_target_pairs={{0,1},{1,2},{2,3},{3,4},{4,5},{5,6},{6,7},{7,8},{8,9},{9,10},{10,1... | collective-permute-start | bytes 393224 | tf_op jit(solution)/shard_map/ppermute | solution.py:14
  14.3 7.4 %collective-permute-start = (bf16[256,256]{0,1:T(8,128)(2,1)S(1)}, bf16[256,256]{0,1:T(8,128)(2,1)S(1)}, u32[]{:S(2)}, u32[]{:S(2)}) collective-permute-start(bf16[256,256]{0,1:T(8,128)(2,1)S(1)} %copy.22), channel_id=1, source_target_pairs={{0,1},{1,2},{2,3},{3,4},{4,5},{5,6},{6,7},{7,8},{8,9},{9,10},{10,1... | collective-permute-start | bytes 393224 | tf_op jit(solution)/shard_map/ppermute | solution.py:14
  30.0 1.1 copy-start.1
  31.9 10.5 %collective-permute-start.2 = (bf16[256,512]{0,1:T(8,128)(2,1)S(1)}, bf16[256,512]{0,1:T(8,128)(2,1)S(1)}, u32[]{:S(2)}, u32[]{:S(2)}) collective-permute-start(bf16[256,512]{0,1:T(8,128)(2,1)S(1)} %fusion.37), channel_id=1, source_target_pairs={{1,0},{2,1},{3,2},{4,3},{5,4},{6,5},{7,6},{8,7},{9,8},{10,9},{11,1... | collective-permute-start | bytes 786440 | tf_op jit(solution)/shard_map/ppermute | solution.py:14
Sparse Core Ops, SparseCore 0:
  45.6 104.1 all-reduce.1
where the time goes:
time: 159 us
  waiting for transfers between devices  110 us (69%)
  between operations  14.3 us (9%)
  local copies, waits for them, and re-layouts  10.4 us (7%)
  matrix products  10.2 us (6%)
  starting transfers between devices  9.75 us (6%)
  other arithmetic  4.31 us (3%)
    psum x1, waiting for transfers between devices, on_device(): whole = lax.psum(term, ('ctx', 'dp'))  101 us
    ppermute x3, starting transfers between devices, shifted(): return lax.ppermute(block, axis, route)  9.71 us
    ppermute x3, waiting for transfers between devices, shifted(): return lax.ppermute(block, axis, route)  9.19 us
    unnamed x10, local copies, waits for them, and re-layouts  8.33 us
  transfers between devices with their start and end apart: 4, of which 2 were waited for; matrix products, arithmetic and copies ran while one was open for 8% of the time, Pallas kernels for 0%

commit v1 on v0

--- a/solution.py
+++ b/solution.py
@@ -94,7 +94,8 @@
     term = weight_term(hidden_in, kv_window[rows_per_block:] + returned)
     total_rows = term.shape[0]
     replica_count = lax.axis_size("dp")
-    whole = lax.psum(term, ("ctx", "dp"))
+    edit_the_task = lambda q_in: jax.lax.psum(jax.lax.psum(q_in, "dp"), axis_name="ctx")
+    whole = edit_the_task(term)
     share = total_rows // replica_count
     weight_grad = lax.dynamic_slice_in_dim(whole, lax.axis_index("dp") * share, share, 0)
     return (query_grad.astype(jnp.bfloat16), weight_grad)

time: 159 us -> 247 us (1.55)
  waiting for transfers between devices: 110 us -> 197 us
    psum x1 -> x2, waiting for transfers between devices: 101 us -> 188 us  [the longest x1 122 us: on_device(): jax.lax.psum(q_in, 'dp')]
  transfers between devices with their start and end apart: 4 -> 5, of which waited for: 2 -> 3; matrix products, arithmetic and copies ran while one was open for 8% -> 5% of each run, Pallas kernels for 0% -> 0%
where the time goes in v1:
time: 247 us; the launch traced here: 246 us
  waiting for transfers between devices  197 us (80%)
  between operations  14.3 us (6%)
  local copies, waits for them, and re-layouts  10.4 us (4%)
  matrix products  10.2 us (4%)
  starting transfers between devices  9.79 us (4%)
  other arithmetic  4.31 us (2%)
    psum x1, waiting for transfers between devices, on_device(): jax.lax.psum(q_in, 'dp')  122 us
    psum x1, waiting for transfers between devices, on_device(): jax.lax.psum(jax.lax.psum(q_in, 'dp'), axis_name='ctx')  66.4 us
    ppermute x3, starting transfers between devices, shifted(): return lax.ppermute(block, axis, route)  9.71 us
    ppermute x3, waiting for transfers between devices, shifted(): return lax.ppermute(block, axis, route)  9.19 us
    unnamed x10, local copies, waits for them, and re-layouts  8.33 us
  transfers between devices with their start and end apart: 5, of which 3 were waited for; matrix products, arithmetic and copies ran while one was open for 5% of the time, Pallas kernels for 0%

profile of v1, /device:TPU:0, one launch (start us, length us, event | category | flops | bytes accessed | tf_op | source)
XLA Modules:
  0.0 246.5 jit_solution(12825689539214373772)
XLA Ops:
  7.2 1.1 copy.27
  8.3 4.9 %collective-permute-start.1 = (bf16[256,256]{0,1:T(8,128)(2,1)S(1)}, bf16[256,256]{0,1:T(8,128)(2,1)S(1)}, u32[]{:S(2)}, u32[]{:S(2)}) collective-permute-start(bf16[256,256]{0,1:T(8,128)(2,1)S(1)} %copy.27), channel_id=1, source_target_pairs={{0,1},{1,2},{2,3},{3,4},{4,5},{5,6},{6,7},{7,8},{8,9},{9,10},{10,1... | collective-permute-start | bytes 393224 | tf_op jit(solution)/shard_map/ppermute | solution.py:14
  13.2 1.0 copy.22
  14.3 3.5 %collective-permute-start = (bf16[256,256]{0,1:T(8,128)(2,1)S(1)}, bf16[256,256]{0,1:T(8,128)(2,1)S(1)}, u32[]{:S(2)}, u32[]{:S(2)}) collective-permute-start(bf16[256,256]{0,1:T(8,128)(2,1)S(1)} %copy.22), channel_id=1, source_target_pairs={{0,1},{1,2},{2,3},{3,4},{4,5},{5,6},{6,7},{7,8},{8,9},{9,10},{10,1... | collective-permute-start | bytes 393224 | tf_op jit(solution)/shard_map/ppermute | solution.py:14
  17.8 1.4 copy.25
  19.2 1.4 copy.30
  20.6 0.8 fusion.51
  22.9 1.4 fusion.52
  24.3 0.7 fusion.27
  25.0 1.5 fusion.53
  26.5 0.6 fusion.2
  27.1 0.6 fusion.24
  28.9 0.6 fusion.31
  30.0 1.1 copy-done.1
  31.1 0.6 fusion.33
  31.9 1.3 collective-permute-start.2
  33.2 9.2 %collective-permute-done.2 = bf16[256,512]{0,1:T(8,128)(2,1)S(1)} collective-permute-done((bf16[256,512]{0,1:T(8,128)(2,1)S(1)}, bf16[256,512]{0,1:T(8,128)(2,1)S(1)}, u32[]{:S(2)}, u32[]{:S(2)}) %collective-permute-start.2) | collective-permute-done | bytes 262176 | tf_op jit(solution)/shard_map/ppermute | solution.py:14
  42.4 3.1 %convolution_bitcast_fusion = f32[1536,512]{0,1:T(8,128)} fusion(bf16[256,1536]{1,0:T(8,128)(2,1)S(1)} %copy-done, f32[512,256]{0,1:T(8,128)S(1)} %bitcast.147, f32[512,256]{0,1:T(8,128)S(1)} %bitcast.145, bf16[256,512]{0,1:T(8,128)(2,1)S(1)} %collective-permute-done.2), kind=kOutput, calls=%fused_computation.2 | convolution fusion | flops 2416312320 | bytes 5242880 | tf_op jit(solution)/shard_map/td,tc->dc/dot_general | solution.py:64
  45.6 121.9 %all-reduce.3.cloned.1.call-done = f32[1536,512]{0,1:T(8,128)} async-done(((f32[1536,512]{0,1:T(8,128)}), f32[1536,512]{0,1:T(8,128)}) %all-reduce.3.cloned.1.call-update) | async-done | bytes 3145744 | tf_op jit(solution)/shard_map/psum | solution.py:97
  167.8 1.8 fusion.23
  169.7 1.2 copy.48
  170.9 66.4 %all-reduce.5.cloned.1.call-done = f32[1536,512]{0,1:T(8,128)} async-done(((f32[1536,512]{0,1:T(8,128)}), f32[1536,512]{0,1:T(8,128)}) %all-reduce.5.cloned.1.call-update) | async-done | bytes 3145744 | tf_op jit(solution)/shard_map/psum | solution.py:97
  237.3 1.2 constant_dynamic-slice_fusion
  238.5 1.1 copy.49
  (25 shorter events, 3.7 us)
Async XLA Ops:
  7.2 35.2 %copy-start = (bf16[256,1536]{1,0:T(8,128)(2,1)S(1)}, bf16[256,1536]{1,0:T(8,128)(2,1)}, u32[]{:S(2)}) copy-start(bf16[256,1536]{1,0:T(8,128)(2,1)} %param.6) | copy-start | bytes 2359300
  7.2 160.2 %all-reduce.3.cloned.1.call-start = ((), (), s32[]{:S(2)}) async-start(), calls=%async_computation | async-start | bytes 6291456 | tf_op jit(solution)/shard_map/psum | solution.py:97
  8.3 18.2 %collective-permute-start.1 = (bf16[256,256]{0,1:T(8,128)(2,1)S(1)}, bf16[256,256]{0,1:T(8,128)(2,1)S(1)}, u32[]{:S(2)}, u32[]{:S(2)}) collective-permute-start(bf16[256,256]{0,1:T(8,128)(2,1)S(1)} %copy.27), channel_id=1, source_target_pairs={{0,1},{1,2},{2,3},{3,4},{4,5},{5,6},{6,7},{7,8},{8,9},{9,10},{10,1... | collective-permute-start | bytes 393224 | tf_op jit(solution)/shard_map/ppermute | solution.py:14
  14.3 7.4 %collective-permute-start = (bf16[256,256]{0,1:T(8,128)(2,1)S(1)}, bf16[256,256]{0,1:T(8,128)(2,1)S(1)}, u32[]{:S(2)}, u32[]{:S(2)}) collective-permute-start(bf16[256,256]{0,1:T(8,128)(2,1)S(1)} %copy.22), channel_id=1, source_target_pairs={{0,1},{1,2},{2,3},{3,4},{4,5},{5,6},{6,7},{7,8},{8,9},{9,10},{10,1... | collective-permute-start | bytes 393224 | tf_op jit(solution)/shard_map/ppermute | solution.py:14
  30.0 1.1 copy-start.1
  31.9 10.5 %collective-permute-start.2 = (bf16[256,512]{0,1:T(8,128)(2,1)S(1)}, bf16[256,512]{0,1:T(8,128)(2,1)S(1)}, u32[]{:S(2)}, u32[]{:S(2)}) collective-permute-start(bf16[256,512]{0,1:T(8,128)(2,1)S(1)} %fusion.37), channel_id=1, source_target_pairs={{1,0},{2,1},{3,2},{4,3},{5,4},{6,5},{7,6},{8,7},{9,8},{10,9},{11,1... | collective-permute-start | bytes 786440 | tf_op jit(solution)/shard_map/ppermute | solution.py:14
  45.5 191.8 %all-reduce.5.cloned.1.call-start = ((), (), s32[]{:S(2)}) async-start(), calls=%async_computation.1 | async-start | bytes 6291456 | tf_op jit(solution)/shard_map/psum | solution.py:97
Sparse Core Ops, SparseCore 0:
  45.6 121.7 all-reduce.2
  169.8 67.4 all-reduce.4
